TPU v7x, 32 devices: a whole 2x2x4 slice. The times are simulated.
32 devices in a mesh: dp: 8 (over y, x, core), fsdp: 4 (over z).
Axes of the slice: x: 2, y: 2, z: 4, core: 2. Of those that a mesh axis runs over, the one named last changes fastest.
Arguments:
- tokens: bfloat16 [18432, 768], P(('dp', 'fsdp')), may hold values from -6 to 6
- image_lengths: int32 [32, 9], P(('dp', 'fsdp')), may hold values from 0 to 576, as said below
- w_qkv: bfloat16 [768, 2304], P('fsdp'), may hold values from -0.21875 to 0.21875
- w_out: bfloat16 [768, 768], P('fsdp'), may hold values from -0.875 to 0.875
- w_up: bfloat16 [768, 3072], P('fsdp'), may hold values from -0.21875 to 0.21875
- w_down: bfloat16 [3072, 768], P('fsdp'), may hold values from -0.109375 to 0.109375
- ln_gain: bfloat16 [2, 768], P(None, 'fsdp'), may hold values from 0.25 to 1.75
- ln_bias: bfloat16 [2, 768], P(None, 'fsdp'), may hold values from -3 to 3
- qk_gain: bfloat16 [2, 768], P(None, 'fsdp'), may hold values from 0.25 to 1.75
- cotangent: bfloat16 [18432, 768], P(('dp', 'fsdp')), may hold values from -6 to 6
Outputs:
- layer_out: bfloat16 [18432, 768], P(('dp', 'fsdp'))
- grad_tokens: bfloat16 [18432, 768], P(('dp', 'fsdp'))
- grad_w_qkv: float32 [768, 2304], P('fsdp')
- grad_w_out: float32 [768, 768], P('fsdp')
- grad_w_up: float32 [768, 3072], P('fsdp')
- grad_w_down: float32 [3072, 768], P('fsdp')
- grad_ln_gain: float32 [2, 768], P(None, 'fsdp')
- grad_ln_bias: float32 [2, 768], P(None, 'fsdp')
- grad_qk_gain: float32 [2, 768], P(None, 'fsdp')
Inputs may be any that keep to these rules, and one draw needn't show every extreme that they name: Each row of image_lengths is either 1 large images of 576 patches, or between 1 and 9 small images of 64 patches; used slots come first, zeros after. Exactly half of the rows hold large images. No image crosses a multiple of 576 rows, and padding lies after the last image.
All inputs are finite; a program needn't handle non-finite values.
Results may differ from a plain program's by a relative error of at most 0.02.
Values may be sent and summed in bfloat16 or wider, within the bound.
No kernel may reach another device: no remote copies, remote signals or barrier semaphores. Data moves between devices by JAX's collectives and lax.ppermute only.
A program may use at most 192 MiB of HBM per device.

v0:
```python
from functools import partial
import jax
import jax.numpy as jnp
from jax import lax
from jax.sharding import PartitionSpec as P

HEADS = 12
HEAD_DIM = 64
PATCH_BIG = 576
epsilon = 1e-06


def layer_norm(v, gain_row, bias_row):
    centre = v - jnp.mean(v, axis=-1, keepdims=True)
    spread = jnp.mean(centre * centre, axis=-1, keepdims=True)
    return centre * lax.rsqrt(spread + epsilon) * gain_row + bias_row


def head_norm(v, gain_row):
    centre = v - jnp.mean(v, axis=-1, keepdims=True)
    spread = jnp.mean(centre * centre, axis=-1, keepdims=True)
    return centre * lax.rsqrt(spread + epsilon) * gain_row


def both_norms(q_in, k_in, q_gain, k_gain):
    return (head_norm(q_in, q_gain), head_norm(k_in, k_gain))


def on_device(
    tokens, image_lengths, w_qkv, w_out, w_up, w_down, ln_gain, ln_bias, qk_gain, cotangent
):
    full_qkv, full_out, full_up, full_down, gain_all, bias_all, qk_all = (
        lax.all_gather(w_qkv, "fsdp", axis=0, tiled=True),
        lax.all_gather(w_out, "fsdp", axis=0, tiled=True),
        lax.all_gather(w_up, "fsdp", axis=0, tiled=True),
        lax.all_gather(w_down, "fsdp", axis=0, tiled=True),
        lax.all_gather(ln_gain, "fsdp", axis=1, tiled=True),
        lax.all_gather(ln_bias, "fsdp", axis=1, tiled=True),
        lax.all_gather(qk_gain, "fsdp", axis=1, tiled=True),
    )
    length = tokens.shape[0]
    model_width = tokens.shape[1]
    blocks = length // PATCH_BIG
    scaling = HEAD_DIM ** (-0.5)
    position = jnp.arange(length, dtype=jnp.int32)
    limits = jnp.cumsum(image_lengths[0])
    segment = jnp.sum((position[:, None] >= limits[None, :]).astype(jnp.int32), axis=1)
    valid_rows = (position < limits[-1]).astype(jnp.float32)[:, None]
    norm_gains = gain_all.astype(jnp.float32)
    biases = bias_all.astype(jnp.float32)
    qk_gains = qk_all.astype(jnp.float32).reshape(2, HEADS, HEAD_DIM)
    inputs = tokens.astype(jnp.float32)
    normed, first_back = jax.vjp(layer_norm, inputs, norm_gains[0], biases[0])
    normed_low = normed.astype(jnp.bfloat16)
    project = jnp.dot(normed_low, full_qkv, preferred_element_type=jnp.float32)
    queries = project[:, :model_width].reshape(length, HEADS, HEAD_DIM)
    keys_raw = project[:, model_width : 2 * model_width].reshape(length, HEADS, HEAD_DIM)
    values_raw = project[:, 2 * model_width :]
    (q_norm, k_norm), norms_back = jax.vjp(both_norms, queries, keys_raw, qk_gains[0], qk_gains[1])
    q_low = q_norm.astype(jnp.bfloat16).reshape(blocks, PATCH_BIG, HEADS, HEAD_DIM)
    k_low = k_norm.astype(jnp.bfloat16).reshape(blocks, PATCH_BIG, HEADS, HEAD_DIM)
    v_low = values_raw.astype(jnp.bfloat16).reshape(blocks, PATCH_BIG, HEADS, HEAD_DIM)
    s_blocks = segment.reshape(blocks, PATCH_BIG)

    def block_scores(q_block, k_block, s_block):
        scores = (
            jnp.einsum("qhd,khd->hqk", q_block, k_block, preferred_element_type=jnp.float32)
            * scaling
        )
        return jnp.where((s_block[:, None] == s_block[None, :])[None], scores, -1e30)

    def attend(members):
        q_block, k_block, v_block, s_block = members
        scores = block_scores(q_block, k_block, s_block)
        row_top = jnp.max(scores, axis=-1, keepdims=True)
        exp_scores = jnp.exp(scores - row_top)
        row_total = jnp.sum(exp_scores, axis=-1, keepdims=True)
        probability = (exp_scores / row_total).astype(jnp.bfloat16)
        mixed_block = jnp.einsum(
            "hqk,khd->qhd", probability, v_block, preferred_element_type=jnp.float32
        )
        return (mixed_block, row_top + jnp.log(row_total))

    mixed_heads, log_total = lax.map(attend, (q_low, k_low, v_low, s_blocks))
    mixed_low = mixed_heads.reshape(length, model_width).astype(jnp.bfloat16)
    residual = inputs + jnp.dot(mixed_low, full_out, preferred_element_type=jnp.float32)
    second, second_back = jax.vjp(layer_norm, residual, norm_gains[1], biases[1])
    second_low = second.astype(jnp.bfloat16)
    up_pre = jnp.dot(second_low, full_up, preferred_element_type=jnp.float32)
    active, gelu_back = jax.vjp(partial(jax.nn.gelu, approximate=False), up_pre)
    active_low = active.astype(jnp.bfloat16)
    output = residual + jnp.dot(active_low, full_down, preferred_element_type=jnp.float32)
    layer_out = (valid_rows * output).astype(jnp.bfloat16)
    back_qkv, back_out, back_up, back_down = (
        lax.all_gather(w_qkv, "fsdp", axis=0, tiled=True),
        lax.all_gather(w_out, "fsdp", axis=0, tiled=True),
        lax.all_gather(w_up, "fsdp", axis=0, tiled=True),
        lax.all_gather(w_down, "fsdp", axis=0, tiled=True),
    )
    upstream = cotangent.astype(jnp.float32) * valid_rows
    up_low = upstream.astype(jnp.bfloat16)
    grad_down = jnp.dot(active_low.T, up_low, preferred_element_type=jnp.float32)
    grad_active = jnp.dot(up_low, back_down.T, preferred_element_type=jnp.float32)
    (grad_pre,) = gelu_back(grad_active)
    pre_low = grad_pre.astype(jnp.bfloat16)
    grad_up = jnp.dot(second_low.T, pre_low, preferred_element_type=jnp.float32)
    grad_second = jnp.dot(pre_low, back_up.T, preferred_element_type=jnp.float32)
    grad_resid, gain_two, bias_two = second_back(grad_second)
    grad_resid = grad_resid + upstream
    resid_low = grad_resid.astype(jnp.bfloat16)
    grad_outw = jnp.dot(mixed_low.T, resid_low, preferred_element_type=jnp.float32)
    grad_mixed = jnp.dot(resid_low, back_out.T, preferred_element_type=jnp.float32)
    grad_mixed = grad_mixed.astype(jnp.bfloat16).reshape(blocks, PATCH_BIG, HEADS, HEAD_DIM)

    def attend_back(members):
        q_block, k_block, v_block, s_block, l_block, d_block = members
        scores = block_scores(q_block, k_block, s_block)
        probability = jnp.exp(scores - l_block)
        prob_low = probability.astype(jnp.bfloat16)
        grad_v = jnp.einsum("hqk,qhd->khd", prob_low, d_block, preferred_element_type=jnp.float32)
        grad_p = jnp.einsum("qhd,khd->hqk", d_block, v_block, preferred_element_type=jnp.float32)
        grad_p = lax.optimization_barrier(grad_p.astype(jnp.bfloat16)).astype(jnp.float32)
        grad_s = probability * (grad_p - jnp.sum(probability * grad_p, axis=-1, keepdims=True))
        s_low = grad_s.astype(jnp.bfloat16)
        grad_q = (
            jnp.einsum("hqk,khd->qhd", s_low, k_block, preferred_element_type=jnp.float32) * scaling
        )
        grad_k = (
            jnp.einsum("hqk,qhd->khd", s_low, q_block, preferred_element_type=jnp.float32) * scaling
        )
        return (grad_q, grad_k, grad_v)

    grad_qn, grad_kn, grad_vn = lax.map(
        attend_back, (q_low, k_low, v_low, s_blocks, log_total, grad_mixed)
    )
    grad_q, grad_k, gain_q, gain_k = norms_back(
        (grad_qn.reshape(length, HEADS, HEAD_DIM), grad_kn.reshape(length, HEADS, HEAD_DIM))
    )
    grad_project = jnp.concatenate(
        [
            grad_q.reshape(length, model_width),
            grad_k.reshape(length, model_width),
            grad_vn.reshape(length, model_width),
        ],
        axis=1,
    ).astype(jnp.bfloat16)
    grad_qkv = jnp.dot(normed_low.T, grad_project, preferred_element_type=jnp.float32)
    grad_normed = jnp.dot(grad_project, back_qkv.T, preferred_element_type=jnp.float32)
    grad_input, gain_one, bias_one = first_back(grad_normed)
    grad_tokens = (grad_input + grad_resid).astype(jnp.bfloat16)
    grad_gain = jnp.stack([gain_one, gain_two])
    grad_bias = jnp.stack([bias_one, bias_two])
    grad_qk = jnp.stack([gain_q.reshape(model_width), gain_k.reshape(model_width)])
    summands = (grad_qkv, grad_outw, grad_up, grad_down, grad_gain, grad_bias, grad_qk)
    pieces = (
        lax.psum_scatter(
            summands[0].astype(jnp.bfloat16), "fsdp", scatter_dimension=0, tiled=True
        ).astype(jnp.float32),
        lax.psum_scatter(
            summands[1].astype(jnp.bfloat16), "fsdp", scatter_dimension=0, tiled=True
        ).astype(jnp.float32),
        lax.psum_scatter(
            summands[2].astype(jnp.bfloat16), "fsdp", scatter_dimension=0, tiled=True
        ).astype(jnp.float32),
        lax.psum_scatter(
            summands[3].astype(jnp.bfloat16), "fsdp", scatter_dimension=0, tiled=True
        ).astype(jnp.float32),
        lax.psum_scatter(
            summands[4].astype(jnp.bfloat16), "fsdp", scatter_dimension=1, tiled=True
        ).astype(jnp.float32),
        lax.psum_scatter(
            summands[5].astype(jnp.bfloat16), "fsdp", scatter_dimension=1, tiled=True
        ).astype(jnp.float32),
        lax.psum_scatter(
            summands[6].astype(jnp.bfloat16), "fsdp", scatter_dimension=1, tiled=True
        ).astype(jnp.float32),
    )
    shares = (
        lax.psum(pieces[0].astype(jnp.bfloat16), "dp").astype(jnp.float32),
        lax.psum(pieces[1].astype(jnp.bfloat16), "dp").astype(jnp.float32),
        lax.psum(pieces[2].astype(jnp.bfloat16), "dp").astype(jnp.float32),
        lax.psum(pieces[3].astype(jnp.bfloat16), "dp").astype(jnp.float32),
        lax.psum(pieces[4].astype(jnp.bfloat16), "dp").astype(jnp.float32),
        lax.psum(pieces[5].astype(jnp.bfloat16), "dp").astype(jnp.float32),
        lax.psum(pieces[6].astype(jnp.bfloat16), "dp").astype(jnp.float32),
    )
    return (
        layer_out,
        grad_tokens,
        shares[0],
        shares[1],
        shares[2],
        shares[3],
        shares[4],
        shares[5],
        shares[6],
    )


def solution(mesh):
    in_specs = (
        P(("dp", "fsdp"), None),
        P(("dp", "fsdp"), None),
        P("fsdp", None),
        P("fsdp", None),
        P("fsdp", None),
        P("fsdp", None),
        P(None, "fsdp"),
        P(None, "fsdp"),
        P(None, "fsdp"),
        P(("dp", "fsdp"), None),
    )
    out_specs = (
        P(("dp", "fsdp"), None),
        P(("dp", "fsdp"), None),
        P("fsdp", None),
        P("fsdp", None),
        P("fsdp", None),
        P("fsdp", None),
        P(None, "fsdp"),
        P(None, "fsdp"),
        P(None, "fsdp"),
    )
    return jax.shard_map(
        on_device, mesh=mesh, in_specs=in_specs, out_specs=out_specs, check_vma=False
    )
```

profile of v0, /device:TPU:0, one launch (start us, length us, event | category | flops | bytes accessed | tf_op | source)
XLA Modules:
  0.0 768.0 jit_solution(16090609015939321576)
XLA Ops:
  11.6 12.7 %all-gather = bf16[4,192,2]{1,2,0:T(2,128)(2,1)S(1)} all-gather(bf16[1,192,2]{1,2,0:T(2,128)(2,1)S(1)} %bitcast.126), channel_id=1, replica_groups=mesh['dp'=8,'fsdp'=4] {'fsdp'}, dimensions={0}, use_global_device_ids=true | all-gather | bytes 3840 | tf_op jit(solution)/shard_map/all_gather | solution.py:37
  24.4 8.1 %all-gather.1 = bf16[4,192,2]{1,2,0:T(2,128)(2,1)S(1)} all-gather(bf16[1,192,2]{1,2,0:T(2,128)(2,1)S(1)} %bitcast.127), channel_id=1, replica_groups=mesh['dp'=8,'fsdp'=4] {'fsdp'}, dimensions={0}, use_global_device_ids=true | all-gather | bytes 3840 | tf_op jit(solution)/shard_map/all_gather | solution.py:38
  32.5 10.7 %all-gather.2 = bf16[4,192,2]{1,2,0:T(2,128)(2,1)S(1)} all-gather(bf16[1,192,2]{1,2,0:T(2,128)(2,1)S(1)} %bitcast.128), channel_id=1, replica_groups=mesh['dp'=8,'fsdp'=4] {'fsdp'}, dimensions={0}, use_global_device_ids=true | all-gather | bytes 3840 | tf_op jit(solution)/shard_map/all_gather | solution.py:39
  44.5 37.8 %all-gather.8.cloned.1.call-done = bf16[768,2304]{1,0:T(8,128)(2,1)} async-done(((bf16[192,2304]{1,0:T(8,128)(2,1)}), bf16[768,2304]{1,0:T(8,128)(2,1)}) %all-gather.8.cloned.1.call-update) | async-done | bytes 3538960 | tf_op jit(solution)/shard_map/all_gather | solution.py:33
  82.3 4.4 fusion.54
  86.9 2.0 fusion.61
  88.9 1.5 copy.68
  90.4 1.9 copy.71
  92.7 2.8 copy.69
  95.5 1.7 reduce_sum.228
  97.2 2.0 multiply_reduce_fusion.1
  99.4 8.1 %fusion.62 = (f32[12,576]{1,0:T(8,128)S(1)}, f32[12,576,576]{1,2,0:T(8,128)}) fusion(f32[576,12,64]{0,2,1:T(8,128)S(1)} %bitcast.95, f32[12,64]{1,0:T(8,128)S(1)} %mul.324, f32[576,12]{0,1:T(8,128)S(1)} %fusion.47, f32[576,12]{0,1:T(8,128)S(1)} %broadcast_multiply_fusion, f32[576,12,64]{0,2,1:T(8,128)S(1)} %bitcast.102, f32[12,64]{1,0:T(8,128)S(1)} %mul.318, ...), kind=kOutput, calls=%fused_computation.139 | convolution fusion | flops 525083904 | bytes 19940352 | tf_op jit(solution)/shard_map/while/body/eval_jaxpr/qhd,khd->hqk/dot_general | solution.py:67
  107.5 8.5 %fusion.3 = f32[12,576]{1,0:T(8,128)S(1)} fusion(f32[12,576,576]{1,2,0:T(8,128)} %get-tuple-element.91, f32[12,576]{1,0:T(8,128)S(1)} %get-tuple-element.90), kind=kLoop, calls=%fused_computation.9 | loop fusion | flops 7955712 | bytes 15980544 | tf_op jit(solution)/shard_map/while/body/eval_jaxpr/reduce_sum | solution.py:77
  116.0 11.4 %fusion.31 = bf16[12,64,576]{2,1,0:T(8,128)(2,1)} fusion(bf16[576,12,64]{0,2,1:T(8,128)(2,1)} %bitcast.109, f32[12,576,576]{1,2,0:T(8,128)} %get-tuple-element.91, f32[12,576]{1,0:T(8,128)S(1)} %fusion.3, f32[12,576]{1,0:T(8,128)S(1)} %get-tuple-element.90), kind=kOutput, calls=%fused_computation.81 | convolution fusion | flops 521994240 | bytes 17750016 | tf_op jit(solution)/shard_map/while/body/eval_jaxpr/hqk,khd->qhd/dot_general | solution.py:79
  127.4 2.6 fusion.63
  131.5 71.6 %all-gather.12.cloned.1.call-done = bf16[768,3072]{1,0:T(8,128)(2,1)} async-done(((bf16[192,3072]{1,0:T(8,128)(2,1)}), bf16[768,3072]{1,0:T(8,128)(2,1)}) %all-gather.12.cloned.1.call-update) | async-done | bytes 4718608 | tf_op jit(solution)/shard_map/all_gather | solution.py:35
  203.1 22.8 %multiply_convert_fusion = (bf16[576,3072]{1,0:T(8,128)(2,1)}, f32[576,3072]{1,0:T(8,128)}, f32[576,3072]{1,0:T(8,128)}) fusion(bf16[768,3072]{1,0:T(8,128)(2,1)} %all-gather.12.cloned.1.call-done, f32[576,768]{1,0:T(8,128)} %copy-done.7, f32[768]{0:T(1024)S(1)} %get-tuple-element.73, f32[768]{0:T(1024)S(1)} %get-tuple-element.102, f32[576]{0:T(1024)S(1)} %fusion.50, ...), kind=kOutput, calls=%fused_computation.17 | convolution fusion | flops 2835136512 | bytes 24193536 | tf_op jit(solution)/shard_map/dot_general | solution.py:89
  225.8 66.5 %all-gather.14.cloned.1.call-done = bf16[3072,768]{1,0:T(8,128)(2,1)} async-done(((bf16[768,768]{1,0:T(8,128)(2,1)}), bf16[3072,768]{1,0:T(8,128)(2,1)}) %all-gather.14.cloned.1.call-update) | async-done | bytes 4718608 | tf_op jit(solution)/shard_map/all_gather | solution.py:36
  292.4 11.3 %add_convert_fusion = bf16[576,3072]{1,0:T(8,128)(2,1)S(1)} fusion(f32[576,3072]{1,0:T(8,128)} %get-tuple-element.87, f32[576,3072]{1,0:T(8,128)} %get-tuple-element.94, bf16[3072,768]{1,0:T(8,128)(2,1)} %all-gather.14.cloned.1.call-done, bf16[576,768]{1,0:T(8,128)(2,1)} %param.19, f32[576]{0:T(1024)S(1)} %fusion.48), kind=kOutput, calls=%fused_computation.16 | convolution fusion | flops 2744008704 | bytes 23300352 | tf_op jit(solution)/shard_map/dot_general | solution.py:103
  303.7 3.3 multiply_reduce_fusion.2
  310.2 2.1 convolution_convert_fusion.4
  312.4 3.3 convolution_convert_fusion.5
  315.8 2.4 copy.73
  318.2 7.6 convolution_convert_fusion
  325.8 12.0 %fusion = f32[12,576]{1,0:T(8,128)S(1)} fusion(bf16[12,576,576]{1,2,0:T(8,128)(2,1)} %convolution_convert_fusion, f32[12,576,576]{1,2,0:T(8,128)} %get-tuple-element.91, f32[12,576]{1,0:T(8,128)S(1)} %log_add_fusion), kind=kLoop, calls=%fused_computation.2 | loop fusion | flops 15918336 | bytes 23943168 | tf_op jit(solution)/shard_map/while/body/eval_jaxpr/reduce_sum | solution.py:123
  338.3 6.6 fusion.2
  345.0 4.0 fusion.23
  349.0 1.8 fusion.24
  356.0 9.2 %fusion.32 = bf16[12,64,576]{2,1,0:T(8,128)(2,1)S(1)} fusion(bf16[576,12,64]{0,2,1:T(8,128)(2,1)S(1)} %bitcast.108, f32[12,576,576]{1,2,0:T(8,128)} %get-tuple-element.91, f32[12,576]{1,0:T(8,128)S(1)} %log_add_fusion), kind=kOutput, calls=%fused_computation.82 | convolution fusion | flops 518012928 | bytes 17722368 | tf_op jit(solution)/shard_map/while/body/eval_jaxpr/hqk,qhd->khd/dot_general | solution.py:120
  366.1 7.4 convolution_convert_fusion.1
  373.5 1.4 copy-done.9
  374.9 7.8 %convolution_convert_fusion.3 = bf16[768,3072]{1,0:T(8,128)(2,1)} fusion(bf16[576,3072]{1,0:T(8,128)(2,1)} %copy-done.38, f32[576,768]{1,0:T(8,128)S(1)} %copy-done.9, f32[768]{0:T(1024)S(1)} %get-tuple-element.73, f32[768]{0:T(1024)S(1)} %get-tuple-element.102, f32[576]{0:T(1024)S(1)} %fusion.50, f32[576]{0:T(1024)S(1)} %broadcast_multiply_fusion.4), kind=kOutput, calls=%fused_computation.34 | convolution fusion | flops 2722480128 | bytes 10037760 | tf_op jit(solution)/shard_map/dot_general | solution.py:106
  383.9 8.0 %convolution_convert_fusion.2 = bf16[3072,768]{1,0:T(8,128)(2,1)} fusion(bf16[576,3072]{1,0:T(8,128)(2,1)} %get-tuple-element.86, bf16[576,768]{1,0:T(8,128)(2,1)S(1)} %copy-done.13, f32[576]{0:T(1024)S(1)} %fusion.48), kind=kOutput, calls=%fused_computation.33 | convolution fusion | flops 2721595392 | bytes 9144576 | tf_op jit(solution)/shard_map/dot_general | solution.py:102
  393.4 5.0 fusion.58
  403.6 35.1 %reduce-scatter.14.cloned.1.call-done = bf16[192,2304]{1,0:T(8,128)(2,1)} async-done(((bf16[768,2304]{1,0:T(8,128)(2,1)}), bf16[192,2304]{1,0:T(8,128)(2,1)}) %reduce-scatter.14.cloned.1.call-update) | async-done | bytes 884752 | tf_op jit(solution)/shard_map/reduce_scatter | solution.py:156
  438.6 87.8 %reduce-scatter.18.cloned.1.call-done = bf16[192,3072]{1,0:T(8,128)(2,1)} async-done(((bf16[768,3072]{1,0:T(8,128)(2,1)}), bf16[192,3072]{1,0:T(8,128)(2,1)}) %reduce-scatter.18.cloned.1.call-update) | async-done | bytes 1179664 | tf_op jit(solution)/shard_map/reduce_scatter | solution.py:162
  526.4 88.1 %reduce-scatter.20.cloned.1.call-done = bf16[768,768]{1,0:T(8,128)(2,1)} async-done(((bf16[3072,768]{1,0:T(8,128)(2,1)}), bf16[768,768]{1,0:T(8,128)(2,1)}) %reduce-scatter.20.cloned.1.call-update) | async-done | bytes 1179664 | tf_op jit(solution)/shard_map/reduce_scatter | solution.py:165
  614.6 3.5 add_convert_fusion.3
  618.1 6.2 multiply_convert_fusion.3
  624.3 13.3 %reduce-scatter.22.cloned.1.call-done = bf16[192,2]{1,0:T(8,128)(2,1)} async-done(((bf16[768,2]{1,0:T(8,128)(2,1)}), bf16[192,2]{1,0:T(8,128)(2,1)}) %reduce-scatter.22.cloned.1.call-update) | async-done | bytes 784
  638.4 19.1 %reduce-scatter.24.cloned.1.call-done = bf16[192,2]{1,0:T(8,128)(2,1)} async-done(((bf16[768,2]{1,0:T(8,128)(2,1)}), bf16[192,2]{1,0:T(8,128)(2,1)}) %reduce-scatter.24.cloned.1.call-update) | async-done | bytes 784
  658.4 19.3 %reduce-scatter.26.cloned.1.call-done = bf16[192,2]{1,0:T(8,128)(2,1)} async-done(((bf16[768,2]{1,0:T(8,128)(2,1)}), bf16[192,2]{1,0:T(8,128)(2,1)}) %reduce-scatter.26.cloned.1.call-update) | async-done | bytes 784
  678.5 12.2 %all-reduce = (bf16[2,192]{1,0:T(2,128)(2,1)S(1)}, bf16[2,192]{1,0:T(2,128)(2,1)S(1)}, bf16[2,192]{1,0:T(2,128)(2,1)S(1)}) all-reduce(bf16[2,192]{1,0:T(2,128)(2,1)S(1)} %copy.84, bf16[2,192]{1,0:T(2,128)(2,1)S(1)} %copy.86, bf16[2,192]{1,0:T(2,128)(2,1)S(1)} %copy.88), channel_id=1, replica_groups=mesh['dp'=8,'fsdp'=4] {'dp'}, use_global_device_ids=true, to_apply=%region_32.33 | all-reduce | flops 1152 | bytes 4608 | tf_op jit(solution)/shard_map/psum | solution.py:183
  692.5 60.7 %all-reduce.4.cloned.1.call-done = (bf16[192,2304]{1,0:T(8,128)(2,1)}, bf16[192,768]{1,0:T(8,128)(2,1)}, bf16[192,3072]{1,0:T(8,128)(2,1)}, bf16[768,768]{1,0:T(8,128)(2,1)}) async-done(((bf16[192,2304]{1,0:T(8,128)(2,1)}, bf16[192,768]{1,0:T(8,128)(2,1)}, bf16[192,3072]{1,0:T(8,128)(2,1)}, bf16[768,768]{1,0:T(8,128)(2,1)}), (bf16[192,2304]{1,0:T(8,128)(2,1)}, bf16[192,768]{1,0:T(8,128)(2,1)}, ...) | async-done | bytes 3538960 | tf_op jit(solution)/shard_map/psum | solution.py:179
  753.2 1.9 convert_element_type.168
  755.1 2.5 convert_element_type.166
  757.6 1.7 convert_element_type.170
  759.3 1.6 convert_element_type.172
  (181 shorter events, 29.8 us)
Async XLA Ops:
  7.2 2.9 copy-start.36
  7.2 4.4 copy-start.32
  7.2 17.2 %copy-start.33 = (bf16[2,192]{1,0:T(2,128)(2,1)S(1)}, bf16[2,192]{1,0:T(2,128)(2,1)}, u32[]{:S(2)}) copy-start(bf16[2,192]{1,0:T(2,128)(2,1)} %param.17) | copy-start | bytes 2308
  7.2 25.3 %copy-start.34 = (bf16[2,192]{1,0:T(2,128)(2,1)S(1)}, bf16[2,192]{1,0:T(2,128)(2,1)}, u32[]{:S(2)}) copy-start(bf16[2,192]{1,0:T(2,128)(2,1)} %param.18) | copy-start | bytes 2308
  7.2 36.2 %copy-start.5 = (bf16[576,768]{1,0:T(8,128)(2,1)S(1)}, bf16[576,768]{1,0:T(8,128)(2,1)}, u32[]{:S(2)}) copy-start(bf16[576,768]{1,0:T(8,128)(2,1)} %param.10) | copy-start | bytes 2654212
  7.2 75.1 %all-gather.8.cloned.1.call-start = ((), (), s32[]{:S(2)}) async-start(), calls=%async_computation.7 | async-start | bytes 4423680 | tf_op jit(solution)/shard_map/all_gather | solution.py:33
  8.0 119.4 %all-gather.10.cloned.1.call-start = ((), (), s32[]{:S(2)}) async-start(), calls=%async_computation.8 | async-start | bytes 1474560 | tf_op jit(solution)/shard_map/all_gather | solution.py:34
  8.7 194.4 %all-gather.12.cloned.1.call-start = ((), (), s32[]{:S(2)}) async-start(), calls=%async_computation.9 | async-start | bytes 5898240 | tf_op jit(solution)/shard_map/all_gather | solution.py:35
  9.4 282.9 %all-gather.14.cloned.1.call-start = ((), (), s32[]{:S(2)}) async-start(), calls=%async_computation.10 | async-start | bytes 5898240 | tf_op jit(solution)/shard_map/all_gather | solution.py:36
  10.0 393.5 %reduce-scatter.16.cloned.1.call-start = ((), (), s32[]{:S(2)}) async-start(), calls=%async_computation.12 | async-start | bytes 1474560 | tf_op jit(solution)/shard_map/reduce_scatter | solution.py:159
  43.7 43.0 %copy-start.22 = (f32[576]{0:T(1024)}, f32[576]{0:T(1024)S(1)}, u32[]{:S(2)}) copy-start(f32[576]{0:T(1024)S(1)} %broadcast_multiply_fusion.5) | copy-start | bytes 6916
  44.1 42.6 %copy-start.24 = (f32[576]{0:T(1024)}, f32[576]{0:T(1024)S(1)}, u32[]{:S(2)}) copy-start(f32[576]{0:T(1024)S(1)} %fusion.28) | copy-start | bytes 6916
  44.1 42.6 %copy-start.28 = (f32[576]{0:T(1024)}, f32[576]{0:T(1024)S(1)}, u32[]{:S(2)}) copy-start(f32[576]{0:T(1024)S(1)} %fusion.49) | copy-start | bytes 6916
  44.5 42.2 %copy-start.26 = (f32[768]{0:T(1024)}, f32[768]{0:T(1024)S(1)}, u32[]{:S(2)}) copy-start(f32[768]{0:T(1024)S(1)} %get-tuple-element.101) | copy-start | bytes 9220
  44.5 42.2 %copy-start.30 = (f32[768]{0:T(1024)}, f32[768]{0:T(1024)S(1)}, u32[]{:S(2)}) copy-start(f32[768]{0:T(1024)S(1)} %get-tuple-element.74) | copy-start | bytes 9220
  97.2 2.2 copy-start
  292.3 11.3 %copy-start.8 = (f32[576,768]{1,0:T(8,128)S(1)}, f32[576,768]{1,0:T(8,128)}, u32[]{:S(2)}) copy-start(f32[576,768]{1,0:T(8,128)} %copy-done.7) | copy-start | bytes 5308420
  292.4 11.3 %copy-start.35 = (bf16[768,3072]{1,0:T(8,128)(2,1)S(1)}, bf16[768,3072]{1,0:T(8,128)(2,1)}, u32[]{:S(2)}) copy-start(bf16[768,3072]{1,0:T(8,128)(2,1)} %all-gather.12.cloned.1.call-done) | copy-start | bytes 14155780
  303.7 3.3 copy-start.38
  307.0 1.9 copy-start.12
  307.8 2.5 copy-start.37
  312.4 126.3 %reduce-scatter.14.cloned.1.call-start = ((), (), s32[]{:S(2)}) async-start(), calls=%async_computation.11 | async-start | bytes 4423680 | tf_op jit(solution)/shard_map/reduce_scatter | solution.py:156
  318.2 19.6 %slice-start = ((s8[17694720]{0:T(1024)(128)(4,1)}), s8[4194304]{0:T(1024)(128)(4,1)S(1)}, s32[]{:S(2)}) async-start(s8[17694720]{0:T(1024)(128)(4,1)} %bitcast.91), calls=%async_computation.19 | async-start | bytes 8388608
  318.2 19.6 %slice-start.1 = ((s8[17694720]{0:T(1024)(128)(4,1)}), s8[917504]{0:T(1024)(128)(4,1)S(1)}, s32[]{:S(2)}) async-start(s8[17694720]{0:T(1024)(128)(4,1)} %bitcast.91), calls=%async_computation.20 | async-start | bytes 1835008
  325.8 12.0 %slice-start.2 = ((s8[17694720]{0:T(1024)(128)(4,1)}), s8[4194304]{0:T(1024)(128)(4,1)S(1)}, s32[]{:S(2)}) async-start(s8[17694720]{0:T(1024)(128)(4,1)} %bitcast.91), calls=%async_computation.21 | async-start | bytes 8388608
  325.8 12.0 %slice-start.3 = ((s8[17694720]{0:T(1024)(128)(4,1)}), s8[4194304]{0:T(1024)(128)(4,1)S(1)}, s32[]{:S(2)}) async-start(s8[17694720]{0:T(1024)(128)(4,1)} %bitcast.91), calls=%async_computation.22 | async-start | bytes 8388608
  325.8 12.5 %slice-start.4 = ((s8[17694720]{0:T(1024)(128)(4,1)}), s8[4194304]{0:T(1024)(128)(4,1)S(1)}, s32[]{:S(2)}) async-start(s8[17694720]{0:T(1024)(128)(4,1)} %bitcast.91), calls=%async_computation.23 | async-start | bytes 8388608
  338.3 6.6 copy-start.1
  349.0 1.9 copy-start.2
  354.4 10.8 %copy-start.16 = (bf16[576,12,64]{0,2,1:T(8,128)(2,1)}, bf16[576,12,64]{0,2,1:T(8,128)(2,1)S(1)}, u32[]{:S(2)}) copy-start(bf16[576,12,64]{0,2,1:T(8,128)(2,1)S(1)} %add_convert_fusion.1) | copy-start | bytes 2654212
  354.4 1.6 copy-start.6
  355.9 9.2 %copy-start.18 = (bf16[576,12,64]{0,2,1:T(8,128)(2,1)}, bf16[576,12,64]{0,2,1:T(8,128)(2,1)S(1)}, u32[]{:S(2)}) copy-start(bf16[576,12,64]{0,2,1:T(8,128)(2,1)S(1)} %add_convert_fusion.2) | copy-start | bytes 2654212
  355.9 10.1 %copy-start.23 = (f32[576]{0:T(1024)S(1)}, f32[576]{0:T(1024)}, u32[]{:S(2)}) copy-start(f32[576]{0:T(1024)} %copy-done.22) | copy-start | bytes 6916
  355.9 10.1 %copy-start.27 = (f32[768]{0:T(1024)S(1)}, f32[768]{0:T(1024)}, u32[]{:S(2)}) copy-start(f32[768]{0:T(1024)} %copy-done.26) | copy-start | bytes 9220
  355.9 10.1 %copy-start.29 = (f32[576]{0:T(1024)S(1)}, f32[576]{0:T(1024)}, u32[]{:S(2)}) copy-start(f32[576]{0:T(1024)} %copy-done.28) | copy-start | bytes 6916
  355.9 10.1 %copy-start.31 = (f32[768]{0:T(1024)S(1)}, f32[768]{0:T(1024)}, u32[]{:S(2)}) copy-start(f32[768]{0:T(1024)} %copy-done.30) | copy-start | bytes 9220
  373.5 152.9 %reduce-scatter.18.cloned.1.call-start = ((), (), s32[]{:S(2)}) async-start(), calls=%async_computation.13 | async-start | bytes 5898240 | tf_op jit(solution)/shard_map/reduce_scatter | solution.py:162
  382.7 231.8 %reduce-scatter.20.cloned.1.call-start = ((), (), s32[]{:S(2)}) async-start(), calls=%async_computation.14 | async-start | bytes 5898240 | tf_op jit(solution)/shard_map/reduce_scatter | solution.py:165
  391.9 245.7 %reduce-scatter.22.cloned.1.call-start = ((), (), s32[]{:S(2)}) async-start(), calls=%async_computation.15 | async-start | bytes 245760
  393.4 5.0 copy-start.25
  401.4 256.1 %reduce-scatter.24.cloned.1.call-start = ((), (), s32[]{:S(2)}) async-start(), calls=%async_computation.16 | async-start | bytes 245760
  402.5 275.1 %reduce-scatter.26.cloned.1.call-start = ((), (), s32[]{:S(2)}) async-start(), calls=%async_computation.17 | async-start | bytes 245760
  402.6 212.0 %copy-start.4 = (f32[576,768]{1,0:T(8,128)S(1)}, f32[576,768]{1,0:T(8,128)}, u32[]{:S(2)}) copy-start(f32[576,768]{1,0:T(8,128)} %copy-done.3) | copy-start | bytes 5308420
  403.5 349.7 %all-reduce.4.cloned.1.call-start = ((), (), s32[]{:S(2)}) async-start(), calls=%async_computation.18 | async-start | bytes 7077888 | tf_op jit(solution)/shard_map/psum | solution.py:179
  614.6 3.5 copy-start.10
  614.6 3.5 copy-start.39
  753.2 4.4 copy-start.15
  757.6 1.7 copy-start.14
  (9 other events, 10.8 us)
Sparse Core Ops, SparseCore 0:
  9.6 72.6 all-gather.7
  83.9 28.9 all-gather.9
  114.4 88.6 all-gather.11
  204.5 87.7 all-gather.13
  312.5 27.7 reduce-scatter.15
  373.6 64.9 reduce-scatter.13
  440.9 85.4 reduce-scatter.17
  528.7 85.7 reduce-scatter.19
  617.4 20.1 reduce-scatter.21
  639.7 17.8 reduce-scatter.23
  659.8 17.8 reduce-scatter.25
  681.2 71.9 all-reduce.3
where the time goes:
time: 772 us; the launch traced here: 768 us
  waiting for transfers between devices  502 us (65%)
  matrix products  126 us (16%)
  other arithmetic  52.6 us (7%)
  blocking collectives  43.7 us (6%)
  local copies, waits for them, and re-layouts  27.9 us (4%)
  between operations  15.2 us (2%)
    reduce_scatter x1, waiting for transfers between devices, on_device(): lax.psum_scatter(summands[3].astype(jnp.bfloat16), 'fsdp', scatter_dimens...  88.1 us
    reduce_scatter x1, waiting for transfers between devices, on_device(): lax.psum_scatter(summands[2].astype(jnp.bfloat16), 'fsdp', scatter_dimens...  87.8 us
    all_gather x1, waiting for transfers between devices, on_device(): lax.all_gather(w_up, 'fsdp', axis=0, tiled=True)  71.6 us
    all_gather x1, waiting for transfers between devices, on_device(): lax.all_gather(w_down, 'fsdp', axis=0, tiled=True)  66.5 us
    psum x1, waiting for transfers between devices, on_device(): lax.psum(pieces[0].astype(jnp.bfloat16), 'dp').astype(jnp.float32)  60.7 us
    unnamed x15, waiting for transfers between devices  54.3 us
    all_gather x1, waiting for transfers between devices, on_device(): lax.all_gather(w_qkv, 'fsdp', axis=0, tiled=True)  37.8 us
    reduce_scatter x1, waiting for transfers between devices, on_device(): lax.psum_scatter(summands[0].astype(jnp.bfloat16), 'fsdp', scatter_dimens...  35.1 us
  transfers between devices with their start and end apart: 12, of which 10 were waited for; matrix products, arithmetic and copies ran while one was open for 22% of the time, Pallas kernels for 0%

commit v1 on v0

--- a/solution.py
+++ b/solution.py
@@ -10,6 +10,28 @@
 epsilon = 1e-06
 
 
+def laid_out(parts, dim):
+    parts = jnp.moveaxis(parts, 0, dim)
+    lengths = parts.shape
+    return parts.reshape(*lengths[:dim], lengths[dim] * lengths[dim + 1], *lengths[dim + 2 :])
+
+
+def collected_by_bits(x, axis):
+    devices = lax.axis_size(axis)
+    blocks = x[None]
+    for level in range(devices.bit_length() - 1):
+        bit = 1 << level
+        theirs = lax.ppermute(blocks, axis, [(i, i ^ bit) for i in range(devices)])
+        both = jnp.stack([blocks, theirs])
+        upper = lax.axis_index(axis) >> level & 1
+        blocks = jnp.where(upper == 0, both, both[::-1]).reshape(-1, *x.shape)
+    return blocks
+
+
+def collect(array, axis, dim):
+    return laid_out(collected_by_bits(array, axis), dim)
+
+
 def layer_norm(v, gain_row, bias_row):
     centre = v - jnp.mean(v, axis=-1, keepdims=True)
     spread = jnp.mean(centre * centre, axis=-1, keepdims=True)
@@ -30,7 +52,7 @@
     tokens, image_lengths, w_qkv, w_out, w_up, w_down, ln_gain, ln_bias, qk_gain, cotangent
 ):
     full_qkv, full_out, full_up, full_down, gain_all, bias_all, qk_all = (
-        lax.all_gather(w_qkv, "fsdp", axis=0, tiled=True),
+        collect(w_qkv, "fsdp", 0),
         lax.all_gather(w_out, "fsdp", axis=0, tiled=True),
         lax.all_gather(w_up, "fsdp", axis=0, tiled=True),
         lax.all_gather(w_down, "fsdp", axis=0, tiled=True),

time: 772 us -> 806 us (1.044)
  blocking collectives: 43.7 us -> 74.5 us
    ppermute x0 -> x2, waiting for transfers between devices: none -> 138 us  [collected_by_bits(): theirs = lax.ppermute(blocks, axis, [(i, i ^ bit) for i in range(devices)])]
    all_gather x1, waiting for transfers between devices: 71.6 us -> 0.02 us  [on_device(): lax.all_gather(w_up, 'fsdp', axis=0, tiled=True)]
    all_gather x1, waiting for transfers between devices: 66.5 us -> 10.4 us  [on_device(): lax.all_gather(w_down, 'fsdp', axis=0, tiled=True)]
    all_gather x1, waiting for transfers between devices: 37.8 us -> 0.01 us  [on_device(): lax.all_gather(w_qkv, 'fsdp', axis=0, tiled=True)]
    all_gather x1, blocking collectives: 12.7 us -> 43.9 us  [on_device(): lax.all_gather(ln_gain, 'fsdp', axis=1, tiled=True)]
    reduce_scatter x1, waiting for transfers between devices: 35.1 us -> 54.5 us  [on_device(): lax.psum_scatter(summands[0].astype(jnp.bfloat16), 'fsdp', scatter_dimens...]
  transfers between devices with their start and end apart: 12 -> 14, of which waited for: 10 -> 9; matrix products, arithmetic and copies ran while one was open for 22% -> 24% of each run, Pallas kernels for 0% -> 0%
where the time goes in v1:
time: 806 us; the launch traced here: 800 us
  waiting for transfers between devices  494 us (61%)
  matrix products  126 us (16%)
  blocking collectives  74.5 us (9%)
  other arithmetic  57.4 us (7%)
  local copies, waits for them, and re-layouts  28.1 us (3%)
  between operations  15.3 us (2%)
    ppermute x2, waiting for transfers between devices, collected_by_bits(): theirs = lax.ppermute(blocks, axis, [(i, i ^ bit) for i in range(devices)])  138 us
    reduce_scatter x1, waiting for transfers between devices, on_device(): lax.psum_scatter(summands[3].astype(jnp.bfloat16), 'fsdp', scatter_dimens...  88.1 us
    reduce_scatter x1, waiting for transfers between devices, on_device(): lax.psum_scatter(summands[2].astype(jnp.bfloat16), 'fsdp', scatter_dimens...  87.8 us
    psum x1, waiting for transfers between devices, on_device(): lax.psum(pieces[0].astype(jnp.bfloat16), 'dp').astype(jnp.float32)  60.7 us
    reduce_scatter x1, waiting for transfers between devices, on_device(): lax.psum_scatter(summands[0].astype(jnp.bfloat16), 'fsdp', scatter_dimens...  54.5 us
    unnamed x15, waiting for transfers between devices  54.4 us
    all_gather x1, blocking collectives, on_device(): lax.all_gather(ln_gain, 'fsdp', axis=1, tiled=True)  43.9 us
    dot_general x1, matrix products, on_device(): up_pre = jnp.dot(second_low, full_up, preferred_element_type=jnp.float32)  22.7 us
  transfers between devices with their start and end apart: 14, of which 9 were waited for; matrix products, arithmetic and copies ran while one was open for 24% of the time, Pallas kernels for 0%

profile of v1, /device:TPU:0, one launch (start us, length us, event | category | flops | bytes accessed | tf_op | source)
XLA Modules:
  0.0 799.8 jit_solution(17368369612413821291)
XLA Ops:
  9.5 3.1 collective-permute-start
  12.7 43.9 %all-gather = bf16[4,192,2]{1,2,0:T(2,128)(2,1)S(1)} all-gather(bf16[1,192,2]{1,2,0:T(2,128)(2,1)S(1)} %bitcast.140), channel_id=1, replica_groups=mesh['dp'=8,'fsdp'=4] {'fsdp'}, dimensions={0}, use_global_device_ids=true | all-gather | bytes 3840 | tf_op jit(solution)/shard_map/all_gather | solution.py:59
  56.7 7.6 all-gather.1
  64.4 10.8 %all-gather.2 = bf16[4,192,2]{1,2,0:T(2,128)(2,1)S(1)} all-gather(bf16[1,192,2]{1,2,0:T(2,128)(2,1)S(1)} %bitcast.142), channel_id=1, replica_groups=mesh['dp'=8,'fsdp'=4] {'fsdp'}, dimensions={0}, use_global_device_ids=true | all-gather | bytes 3840 | tf_op jit(solution)/shard_map/all_gather | solution.py:61
  80.4 137.7 %collective-permute-done.1 = bf16[2,192,2304]{2,1,0:T(8,128)(2,1)S(1)} collective-permute-done((bf16[2,192,2304]{2,1,0:T(8,128)(2,1)S(1)}, bf16[2,192,2304]{2,1,0:T(8,128)(2,1)S(1)}, u32[]{:S(2)}, u32[]{:S(2)}) %collective-permute-start.1) | collective-permute-done | bytes 1769504 | tf_op jit(solution)/shard_map/ppermute | solution.py:24
  219.1 2.4 fusion.56
  221.6 2.0 fusion.63
  224.6 1.9 copy.71
  226.9 2.8 copy.69
  229.7 1.7 reduce_sum.228
  231.4 1.8 multiply_reduce_fusion.1
  233.2 2.4 copy.68
  235.7 11.3 %fusion.64 = (f32[12,576]{1,0:T(8,128)S(1)}, f32[12,576,576]{1,2,0:T(8,128)}) fusion(f32[576,12,64]{0,2,1:T(8,128)S(1)} %bitcast.104, f32[12,64]{1,0:T(8,128)S(1)} %mul.324, f32[576,12]{0,1:T(8,128)S(1)} %get-tuple-element.104, f32[576,12]{0,1:T(8,128)S(1)} %broadcast_multiply_fusion, f32[576,12,64]{0,2,1:T(8,128)} %bitcast.111, f32[12,64]{1,0:T(8,128)S(1)} %mul.318, ...), kind=kOutput, calls=%fused_computation.145 | convolution fusion | flops 525083904 | bytes 19940352 | tf_op jit(solution)/shard_map/while/body/eval_jaxpr/qhd,khd->hqk/dot_general | solution.py:89
  246.9 8.6 %fusion.3 = f32[12,576]{1,0:T(8,128)S(1)} fusion(f32[12,576,576]{1,2,0:T(8,128)} %get-tuple-element.93, f32[12,576]{1,0:T(8,128)S(1)} %get-tuple-element.92), kind=kLoop, calls=%fused_computation.9 | loop fusion | flops 7955712 | bytes 15980544 | tf_op jit(solution)/shard_map/while/body/eval_jaxpr/reduce_sum | solution.py:99
  255.6 10.7 %fusion.31 = bf16[12,64,576]{2,1,0:T(8,128)(2,1)} fusion(bf16[576,12,64]{0,2,1:T(8,128)(2,1)} %bitcast.118, f32[12,576,576]{1,2,0:T(8,128)} %get-tuple-element.93, f32[12,576]{1,0:T(8,128)S(1)} %fusion.3, f32[12,576]{1,0:T(8,128)S(1)} %get-tuple-element.92), kind=kOutput, calls=%fused_computation.85 | convolution fusion | flops 521994240 | bytes 17750016 | tf_op jit(solution)/shard_map/while/body/eval_jaxpr/hqk,khd->qhd/dot_general | solution.py:101
  266.2 2.6 fusion.65
  270.4 22.7 %multiply_convert_fusion = (bf16[576,3072]{1,0:T(8,128)(2,1)}, f32[576,3072]{1,0:T(8,128)}, f32[576,3072]{1,0:T(8,128)}) fusion(bf16[768,3072]{1,0:T(8,128)(2,1)} %all-gather.10.cloned.1.call-done, f32[576,768]{1,0:T(8,128)} %copy-done.7, f32[768]{0:T(1024)S(1)} %get-tuple-element.73, f32[768]{0:T(1024)S(1)} %get-tuple-element.71, f32[576]{0:T(1024)S(1)} %fusion.52, ...), kind=kOutput, calls=%fused_computation.17 | convolution fusion | flops 2835136512 | bytes 24193536 | tf_op jit(solution)/shard_map/dot_general | solution.py:111
  293.1 10.4 %all-gather.12.cloned.1.call-done = bf16[3072,768]{1,0:T(8,128)(2,1)} async-done(((bf16[768,768]{1,0:T(8,128)(2,1)}), bf16[3072,768]{1,0:T(8,128)(2,1)}) %all-gather.12.cloned.1.call-update) | async-done | bytes 4718608 | tf_op jit(solution)/shard_map/all_gather | solution.py:58
  303.5 11.5 %add_convert_fusion = bf16[576,3072]{1,0:T(8,128)(2,1)S(1)} fusion(f32[576,3072]{1,0:T(8,128)} %get-tuple-element.87, f32[576,3072]{1,0:T(8,128)} %get-tuple-element.96, bf16[3072,768]{1,0:T(8,128)(2,1)} %all-gather.12.cloned.1.call-done, bf16[576,768]{1,0:T(8,128)(2,1)} %param.19, f32[576]{0:T(1024)S(1)} %fusion.50), kind=kOutput, calls=%fused_computation.16 | convolution fusion | flops 2744008704 | bytes 23300352 | tf_op jit(solution)/shard_map/dot_general | solution.py:125
  315.0 3.3 multiply_reduce_fusion.2
  321.6 1.8 convolution_convert_fusion.5
  323.4 2.3 copy.73
  325.7 7.6 convolution_convert_fusion
  333.3 12.0 %fusion = f32[12,576]{1,0:T(8,128)S(1)} fusion(bf16[12,576,576]{1,2,0:T(8,128)(2,1)} %convolution_convert_fusion, f32[12,576,576]{1,2,0:T(8,128)} %get-tuple-element.93, f32[12,576]{1,0:T(8,128)S(1)} %log_add_fusion), kind=kLoop, calls=%fused_computation.2 | loop fusion | flops 15918336 | bytes 23943168 | tf_op jit(solution)/shard_map/while/body/eval_jaxpr/reduce_sum | solution.py:145
  345.7 6.8 fusion.2
  352.5 1.8 fusion.24
  357.1 4.0 fusion.23
  361.1 2.1 convolution_convert_fusion.4
  363.3 2.7 fusion.21
  366.1 3.0 add_convert_fusion.2
  370.7 9.1 %fusion.32 = bf16[12,64,576]{2,1,0:T(8,128)(2,1)S(1)} fusion(bf16[576,12,64]{0,2,1:T(8,128)(2,1)S(1)} %bitcast.117, f32[12,576,576]{1,2,0:T(8,128)} %get-tuple-element.93, f32[12,576]{1,0:T(8,128)S(1)} %log_add_fusion), kind=kOutput, calls=%fused_computation.86 | convolution fusion | flops 518012928 | bytes 17722368 | tf_op jit(solution)/shard_map/while/body/eval_jaxpr/hqk,qhd->khd/dot_general | solution.py:142
  380.8 7.2 convolution_convert_fusion.1
  388.1 1.4 copy-done.9
  389.5 7.8 convolution_convert_fusion.3
  398.4 8.0 %convolution_convert_fusion.2 = bf16[3072,768]{1,0:T(8,128)(2,1)} fusion(bf16[576,3072]{1,0:T(8,128)(2,1)} %get-tuple-element.86, bf16[576,768]{1,0:T(8,128)(2,1)S(1)} %copy-done.15, f32[576]{0:T(1024)S(1)} %fusion.50), kind=kOutput, calls=%fused_computation.34 | convolution fusion | flops 2721595392 | bytes 9144576 | tf_op jit(solution)/shard_map/dot_general | solution.py:124
  407.6 5.8 fusion.60
  416.3 54.5 %reduce-scatter.14.cloned.1.call-done = bf16[192,2304]{1,0:T(8,128)(2,1)} async-done(((bf16[768,2304]{1,0:T(8,128)(2,1)}), bf16[192,2304]{1,0:T(8,128)(2,1)}) %reduce-scatter.14.cloned.1.call-update) | async-done | bytes 884752 | tf_op jit(solution)/shard_map/reduce_scatter | solution.py:178
  470.8 87.8 %reduce-scatter.18.cloned.1.call-done = bf16[192,3072]{1,0:T(8,128)(2,1)} async-done(((bf16[768,3072]{1,0:T(8,128)(2,1)}), bf16[192,3072]{1,0:T(8,128)(2,1)}) %reduce-scatter.18.cloned.1.call-update) | async-done | bytes 1179664 | tf_op jit(solution)/shard_map/reduce_scatter | solution.py:184
  558.5 88.1 %reduce-scatter.20.cloned.1.call-done = bf16[768,768]{1,0:T(8,128)(2,1)} async-done(((bf16[3072,768]{1,0:T(8,128)(2,1)}), bf16[768,768]{1,0:T(8,128)(2,1)}) %reduce-scatter.20.cloned.1.call-update) | async-done | bytes 1179664 | tf_op jit(solution)/shard_map/reduce_scatter | solution.py:187
  646.8 3.5 add_convert_fusion.3
  650.2 6.2 multiply_convert_fusion.3
  656.4 12.7 %reduce-scatter.26.cloned.1.call-done = bf16[192,2]{1,0:T(8,128)(2,1)} async-done(((bf16[768,2]{1,0:T(8,128)(2,1)}), bf16[192,2]{1,0:T(8,128)(2,1)}) %reduce-scatter.26.cloned.1.call-update) | async-done | bytes 784
  670.0 19.7 %reduce-scatter.24.cloned.1.call-done = bf16[192,2]{1,0:T(8,128)(2,1)} async-done(((bf16[768,2]{1,0:T(8,128)(2,1)}), bf16[192,2]{1,0:T(8,128)(2,1)}) %reduce-scatter.24.cloned.1.call-update) | async-done | bytes 784
  690.5 19.8 %reduce-scatter.22.cloned.1.call-done = bf16[192,2]{1,0:T(8,128)(2,1)} async-done(((bf16[768,2]{1,0:T(8,128)(2,1)}), bf16[192,2]{1,0:T(8,128)(2,1)}) %reduce-scatter.22.cloned.1.call-update) | async-done | bytes 784
  711.2 12.2 %all-reduce = (bf16[2,192]{1,0:T(2,128)(2,1)S(1)}, bf16[2,192]{1,0:T(2,128)(2,1)S(1)}, bf16[2,192]{1,0:T(2,128)(2,1)S(1)}) all-reduce(bf16[2,192]{1,0:T(2,128)(2,1)S(1)} %copy.84, bf16[2,192]{1,0:T(2,128)(2,1)S(1)} %copy.86, bf16[2,192]{1,0:T(2,128)(2,1)S(1)} %copy.88), channel_id=1, replica_groups=mesh['dp'=8,'fsdp'=4] {'dp'}, use_global_device_ids=true, to_apply=%region_32.33 | all-reduce | flops 1152 | bytes 4608 | tf_op jit(solution)/shard_map/psum | solution.py:205
  725.2 60.7 %all-reduce.4.cloned.1.call-done = (bf16[192,2304]{1,0:T(8,128)(2,1)}, bf16[192,768]{1,0:T(8,128)(2,1)}, bf16[192,3072]{1,0:T(8,128)(2,1)}, bf16[768,768]{1,0:T(8,128)(2,1)}) async-done(((bf16[192,2304]{1,0:T(8,128)(2,1)}, bf16[192,768]{1,0:T(8,128)(2,1)}, bf16[192,3072]{1,0:T(8,128)(2,1)}, bf16[768,768]{1,0:T(8,128)(2,1)}), (bf16[192,2304]{1,0:T(8,128)(2,1)}, bf16[192,768]{1,0:T(8,128)(2,1)}, ...) | async-done | bytes 3538960 | tf_op jit(solution)/shard_map/psum | solution.py:201
  785.9 3.0 convert_element_type.170
  788.9 1.6 convert_element_type.172
  (197 shorter events, 32.0 us)
Async XLA Ops:
  7.2 69.1 %copy-start.13 = (bf16[192,2304]{1,0:T(8,128)(2,1)S(1)}, bf16[192,2304]{1,0:T(8,128)(2,1)}, u32[]{:S(2)}) copy-start(bf16[192,2304]{1,0:T(8,128)(2,1)} %param.12) | copy-start | bytes 2654212
  7.2 5.5 copy-start.35
  7.2 49.5 %copy-start.36 = (bf16[2,192]{1,0:T(2,128)(2,1)S(1)}, bf16[2,192]{1,0:T(2,128)(2,1)}, u32[]{:S(2)}) copy-start(bf16[2,192]{1,0:T(2,128)(2,1)} %param.17) | copy-start | bytes 2308
  7.2 57.2 %copy-start.37 = (bf16[2,192]{1,0:T(2,128)(2,1)S(1)}, bf16[2,192]{1,0:T(2,128)(2,1)}, u32[]{:S(2)}) copy-start(bf16[2,192]{1,0:T(2,128)(2,1)} %param.18) | copy-start | bytes 2308
  7.2 68.2 %copy-start.40 = (s32[1,9]{1,0:T(1,128)S(1)}, s32[1,9]{1,0:T(1,128)}, u32[]{:S(2)}) copy-start(s32[1,9]{1,0:T(1,128)} %param.11) | copy-start | bytes 112
  7.2 259.0 %all-gather.8.cloned.1.call-start = ((), (), s32[]{:S(2)}) async-start(), calls=%async_computation.7 | async-start | bytes 1474560 | tf_op jit(solution)/shard_map/all_gather | solution.py:56
  8.0 262.4 %all-gather.10.cloned.1.call-start = ((), (), s32[]{:S(2)}) async-start(), calls=%async_computation.8 | async-start | bytes 5898240 | tf_op jit(solution)/shard_map/all_gather | solution.py:57
  8.7 294.8 %all-gather.12.cloned.1.call-start = ((), (), s32[]{:S(2)}) async-start(), calls=%async_computation.9 | async-start | bytes 5898240 | tf_op jit(solution)/shard_map/all_gather | solution.py:58
  9.5 398.1 %all-gather.14.cloned.1.call-start = ((), (), s32[]{:S(2)}) async-start(), calls=%async_computation.10 | async-start | bytes 4423680 | tf_op jit(solution)/shard_map/all_gather | solution.py:117
  9.5 66.8 %collective-permute-start = (bf16[1,192,2304]{2,1,0:T(8,128)(2,1)S(1)}, bf16[1,192,2304]{2,1,0:T(8,128)(2,1)S(1)}, u32[]{:S(2)}, u32[]{:S(2)}) collective-permute-start(bf16[1,192,2304]{2,1,0:T(8,128)(2,1)S(1)} %bitcast.121), channel_id=1, source_target_pairs={{0,1},{1,0},{2,3},{3,2},{4,5},{5,4},{6,7},{7,6},{8,9},{9,8},{10,11... | collective-permute-start | bytes 2654216 | tf_op jit(solution)/shard_map/ppermute | solution.py:24
  12.7 403.7 %reduce-scatter.16.cloned.1.call-start = ((), (), s32[]{:S(2)}) async-start(), calls=%async_computation.12 | async-start | bytes 1474560 | tf_op jit(solution)/shard_map/reduce_scatter | solution.py:181
  76.3 142.8 %copy-start.29 = (f32[768]{0:T(1024)}, f32[768]{0:T(1024)S(1)}, u32[]{:S(2)}) copy-start(f32[768]{0:T(1024)S(1)} %get-tuple-element.72) | copy-start | bytes 9220
  76.8 141.3 %collective-permute-start.1 = (bf16[2,192,2304]{2,1,0:T(8,128)(2,1)S(1)}, bf16[2,192,2304]{2,1,0:T(8,128)(2,1)S(1)}, u32[]{:S(2)}, u32[]{:S(2)}) collective-permute-start(bf16[2,192,2304]{2,1,0:T(8,128)(2,1)S(1)} %get-tuple-element.91), channel_id=1, source_target_pairs={{0,2},{1,3},{2,0},{3,1},{4,6},{5,7},{6,4},{7,5},{8,10},{9,11},{10,... | collective-permute-start | bytes 5308424 | tf_op jit(solution)/shard_map/ppermute | solution.py:24
  78.7 140.4 %copy-start.33 = (f32[768]{0:T(1024)}, f32[768]{0:T(1024)S(1)}, u32[]{:S(2)}) copy-start(f32[768]{0:T(1024)S(1)} %get-tuple-element.74) | copy-start | bytes 9220
  79.0 140.1 %copy-start.25 = (f32[576]{0:T(1024)}, f32[576]{0:T(1024)S(1)}, u32[]{:S(2)}) copy-start(f32[576]{0:T(1024)S(1)} %broadcast_multiply_fusion.5) | copy-start | bytes 6916
  79.4 139.0 %copy-start.27 = (f32[576]{0:T(1024)}, f32[576]{0:T(1024)S(1)}, u32[]{:S(2)}) copy-start(f32[576]{0:T(1024)S(1)} %fusion.28) | copy-start | bytes 6916
  79.5 139.7 %copy-start.31 = (f32[576]{0:T(1024)}, f32[576]{0:T(1024)S(1)}, u32[]{:S(2)}) copy-start(f32[576]{0:T(1024)S(1)} %fusion.51) | copy-start | bytes 6916
  303.5 11.5 %copy-start.8 = (f32[576,768]{1,0:T(8,128)S(1)}, f32[576,768]{1,0:T(8,128)}, u32[]{:S(2)}) copy-start(f32[576,768]{1,0:T(8,128)} %copy-done.7) | copy-start | bytes 5308420
  303.5 11.5 %copy-start.38 = (bf16[768,3072]{1,0:T(8,128)(2,1)S(1)}, bf16[768,3072]{1,0:T(8,128)(2,1)}, u32[]{:S(2)}) copy-start(bf16[768,3072]{1,0:T(8,128)(2,1)} %all-gather.10.cloned.1.call-done) | copy-start | bytes 14155780
  315.0 3.3 copy-start.42
  319.1 2.5 copy-start.39
  325.7 19.6 %slice-start = ((s8[17694720]{0:T(1024)(128)(4,1)}), s8[4194304]{0:T(1024)(128)(4,1)S(1)}, s32[]{:S(2)}) async-start(s8[17694720]{0:T(1024)(128)(4,1)} %bitcast.100), calls=%async_computation.19 | async-start | bytes 8388608
  325.7 19.6 %slice-start.1 = ((s8[17694720]{0:T(1024)(128)(4,1)}), s8[917504]{0:T(1024)(128)(4,1)S(1)}, s32[]{:S(2)}) async-start(s8[17694720]{0:T(1024)(128)(4,1)} %bitcast.100), calls=%async_computation.20 | async-start | bytes 1835008
  333.3 12.0 %slice-start.2 = ((s8[17694720]{0:T(1024)(128)(4,1)}), s8[4194304]{0:T(1024)(128)(4,1)S(1)}, s32[]{:S(2)}) async-start(s8[17694720]{0:T(1024)(128)(4,1)} %bitcast.100), calls=%async_computation.21 | async-start | bytes 8388608
  333.3 12.0 %slice-start.3 = ((s8[17694720]{0:T(1024)(128)(4,1)}), s8[4194304]{0:T(1024)(128)(4,1)S(1)}, s32[]{:S(2)}) async-start(s8[17694720]{0:T(1024)(128)(4,1)} %bitcast.100), calls=%async_computation.22 | async-start | bytes 8388608
  333.3 12.4 %slice-start.4 = ((s8[17694720]{0:T(1024)(128)(4,1)}), s8[4194304]{0:T(1024)(128)(4,1)S(1)}, s32[]{:S(2)}) async-start(s8[17694720]{0:T(1024)(128)(4,1)} %bitcast.100), calls=%async_computation.23 | async-start | bytes 8388608
  345.7 6.8 copy-start
  357.0 4.1 copy-start.21
  357.1 4.1 copy-start.41
  366.0 104.8 %reduce-scatter.14.cloned.1.call-start = ((), (), s32[]{:S(2)}) async-start(), calls=%async_computation.11 | async-start | bytes 4423680 | tf_op jit(solution)/shard_map/reduce_scatter | solution.py:178
  366.1 3.0 copy-start.2
  369.1 10.7 %copy-start.17 = (bf16[576,12,64]{0,2,1:T(8,128)(2,1)}, bf16[576,12,64]{0,2,1:T(8,128)(2,1)S(1)}, u32[]{:S(2)}) copy-start(bf16[576,12,64]{0,2,1:T(8,128)(2,1)S(1)} %add_convert_fusion.2) | copy-start | bytes 2654212
  370.7 9.2 %copy-start.18 = (bf16[576,12,64]{0,2,1:T(8,128)(2,1)}, bf16[576,12,64]{0,2,1:T(8,128)(2,1)S(1)}, u32[]{:S(2)}) copy-start(bf16[576,12,64]{0,2,1:T(8,128)(2,1)S(1)} %add_convert_fusion.1) | copy-start | bytes 2654212
  370.7 10.1 %copy-start.26 = (f32[576]{0:T(1024)S(1)}, f32[576]{0:T(1024)}, u32[]{:S(2)}) copy-start(f32[576]{0:T(1024)} %copy-done.25) | copy-start | bytes 6916
  370.7 10.1 %copy-start.30 = (f32[768]{0:T(1024)S(1)}, f32[768]{0:T(1024)}, u32[]{:S(2)}) copy-start(f32[768]{0:T(1024)} %copy-done.29) | copy-start | bytes 9220
  370.7 10.1 %copy-start.32 = (f32[576]{0:T(1024)S(1)}, f32[576]{0:T(1024)}, u32[]{:S(2)}) copy-start(f32[576]{0:T(1024)} %copy-done.31) | copy-start | bytes 6916
  370.7 10.1 %copy-start.34 = (f32[768]{0:T(1024)S(1)}, f32[768]{0:T(1024)}, u32[]{:S(2)}) copy-start(f32[768]{0:T(1024)} %copy-done.33) | copy-start | bytes 9220
  388.0 170.5 %reduce-scatter.18.cloned.1.call-start = ((), (), s32[]{:S(2)}) async-start(), calls=%async_computation.13 | async-start | bytes 5898240 | tf_op jit(solution)/shard_map/reduce_scatter | solution.py:184
  397.3 249.4 %reduce-scatter.20.cloned.1.call-start = ((), (), s32[]{:S(2)}) async-start(), calls=%async_computation.14 | async-start | bytes 5898240 | tf_op jit(solution)/shard_map/reduce_scatter | solution.py:187
  406.5 262.6 %reduce-scatter.26.cloned.1.call-start = ((), (), s32[]{:S(2)}) async-start(), calls=%async_computation.17 | async-start | bytes 245760
  407.6 5.9 copy-start.28
  413.5 276.2 %reduce-scatter.24.cloned.1.call-start = ((), (), s32[]{:S(2)}) async-start(), calls=%async_computation.16 | async-start | bytes 245760
  415.3 295.1 %reduce-scatter.22.cloned.1.call-start = ((), (), s32[]{:S(2)}) async-start(), calls=%async_computation.15 | async-start | bytes 245760
  415.4 231.4 %copy-start.4 = (f32[576,768]{1,0:T(8,128)S(1)}, f32[576,768]{1,0:T(8,128)}, u32[]{:S(2)}) copy-start(f32[576,768]{1,0:T(8,128)} %copy-done.3) | copy-start | bytes 5308420
  416.2 369.6 %all-reduce.4.cloned.1.call-start = ((), (), s32[]{:S(2)}) async-start(), calls=%async_computation.18 | async-start | bytes 7077888 | tf_op jit(solution)/shard_map/psum | solution.py:201
  646.7 3.5 copy-start.10
  646.7 3.5 copy-start.43
  785.9 3.0 copy-start.16
  (15 other events, 22.6 us)
Sparse Core Ops, SparseCore 0:
  9.6 41.5 all-gather.7
  52.8 161.4 all-gather.9
  215.9 87.5 all-gather.11
  304.9 68.3 all-gather.13
  375.5 27.9 reduce-scatter.15
  405.6 65.1 reduce-scatter.13
  473.1 85.4 reduce-scatter.17
  560.8 85.7 reduce-scatter.19
  649.0 20.1 reduce-scatter.25
  671.8 17.8 reduce-scatter.23
  692.5 17.8 reduce-scatter.21
  713.9 71.9 all-reduce.3
